TPU v7x, 256 devices: a whole 4x4x8 slice. The times are simulated.
256 devices in a mesh: svc: 32 (over y_lo, z, core), tm: 8 (over y_hi, x).
Axes of the slice: x: 4, y: 4 (y_hi: 2, y_lo: 2; y = y_hi * 2 + y_lo), z: 8, core: 2. Of those that a mesh axis runs over, the one named last changes fastest.
Arguments:
- metrics: bfloat16 [8192, 4096], P('svc', 'tm'), may hold values from -15 to 15
- band_starts: int32 [4], replicated, may hold values from 1 to 2015
Outputs:
- cross: bfloat16 [4, 2, 8192, 8192], P(None, None, 'svc', 'tm')
- coherence: float32 [4, 8192, 8192], P(None, 'svc', 'tm')
Inputs may be any that keep to these rules, and one draw needn't show every extreme that they name: `band_starts`: each band covers 32 consecutive bins starting at its entry.
All inputs are finite; a program needn't handle non-finite values.
Results may differ from a plain program's by a relative error of at most 0.0066.
Values may be sent and summed in bfloat16 or wider, within the bound.
No kernel may reach another device: no remote copies, remote signals or barrier semaphores. Data moves between devices by JAX's collectives and lax.ppermute only.
A program may use at most 64 MiB of HBM per device.

v0:
```python
import jax
import jax.numpy as jnp
from jax import lax
from jax.sharding import PartitionSpec as P

TLEN = 4096
BANDS = 4
BINS = 32
epsilon = 1e-06


def make_table(minutes, band_starts):
    offsets = jnp.arange(BINS, dtype=jnp.int32)
    freqs = band_starts[:, None] + offsets[None, :]
    phase_index = minutes[:, None, None] * freqs[None, :, :] % TLEN
    phases = 2.0 * jnp.pi / TLEN * phase_index.astype(jnp.float32)
    norm = 1.0 / jnp.sqrt(jnp.float32(TLEN))
    stacked = jnp.stack([jnp.cos(phases) * norm, -jnp.sin(phases) * norm], axis=2)
    return stacked.reshape(minutes.shape[0], BANDS * 2 * BINS).astype(jnp.bfloat16)


def band_products(row_spec, col_spec):
    swapped = jnp.concatenate([row_spec[:, BINS:], -row_spec[:, :BINS]], axis=1)
    dims = (((1,), (1,)), ((), ()))
    real_part = lax.dot_general(row_spec, col_spec, dims, preferred_element_type=jnp.float32) / BINS
    imag_part = lax.dot_general(swapped, col_spec, dims, preferred_element_type=jnp.float32) / BINS
    row_power = jnp.sum(jnp.square(row_spec.astype(jnp.float32)), axis=1) / BINS
    col_power = jnp.sum(jnp.square(col_spec.astype(jnp.float32)), axis=1) / BINS
    coherence = (real_part * real_part + imag_part * imag_part) / (
        (row_power[:, None] + epsilon) * (col_power[None, :] + epsilon)
    )
    cross = jnp.stack([real_part, imag_part], axis=0).astype(jnp.bfloat16)
    return (cross, coherence)


def body(metrics, band_starts):
    row_count = metrics.shape[0]
    local_minutes = metrics.shape[1]
    time_index = lax.axis_index("tm")
    minutes = time_index * local_minutes + jnp.arange(local_minutes, dtype=jnp.int32)
    dft_table = make_table(minutes, band_starts)
    partial_value = jnp.dot(metrics, dft_table, preferred_element_type=jnp.float32)
    spectra = lax.psum(partial_value, "tm").astype(jnp.bfloat16)
    owners = lax.axis_size("svc") // lax.axis_size("tm")
    col_count = row_count * owners
    gathered = lax.all_gather(spectra, "svc", axis=0, tiled=True)
    columns_panel = lax.dynamic_slice_in_dim(gathered, time_index * col_count, col_count, 0)
    cross_list = []
    coherence_list = []
    for band in range(BANDS):
        offset = band * 2 * BINS
        row_spec = spectra[:, offset : offset + 2 * BINS]
        col_spec = columns_panel[:, offset : offset + 2 * BINS]
        cross, coherence = band_products(row_spec, col_spec)
        cross_list.append(cross)
        coherence_list.append(coherence)
    return (jnp.stack(cross_list, axis=0), jnp.stack(coherence_list, axis=0))


def solution(mesh):
    return jax.shard_map(
        body,
        mesh=mesh,
        in_specs=(P("svc", "tm"), P()),
        out_specs=(P(None, None, "svc", "tm"), P(None, "svc", "tm")),
        check_vma=False,
    )
```

profile of v0, /device:TPU:1, one launch (start us, length us, event | category | flops | bytes accessed | tf_op | source)
XLA Modules:
  0.0 150.9 jit_solution(4337779228758525286)
XLA Ops:
  7.2 0.0 copy-start
  7.2 0.0 all-gather.2.cloned.1.call-start
  7.2 0.8 iota_add_fusion
  8.0 1.2 multiply_convert_fusion.1
  9.3 0.0 copy-done
  9.3 0.3 convolution_bitcast_fusion
  9.5 38.9 %all-reduce.1 = bf16[256,256]{0,1:T(8,128)(2,1)} all-reduce(f32[256,256]{0,1:T(8,128)S(1)} %convolution_bitcast_fusion), channel_id=1, replica_groups=mesh['svc'=32,'tm'=8] {'tm'}, use_global_device_ids=true, to_apply=%region_0.1 | all-reduce | flops 65536 | bytes 393216 | tf_op jit(solution)/shard_map/psum | solution.py:43
  48.5 0.0 copy-start.1
  48.5 0.0 all-gather.2.cloned.1.call-update
  48.5 0.9 multiply_reduce_fusion.7
  49.4 0.9 fusion.33
  50.3 77.2 %all-gather.2.cloned.1.call-done = bf16[8192,256]{0,1:T(8,128)(2,1)} async-done(((bf16[256,256]{0,1:T(8,128)(2,1)}), bf16[8192,256]{0,1:T(8,128)(2,1)}) %all-gather.2.cloned.1.call-update) | async-done | bytes 4194320 | tf_op jit(solution)/shard_map/all_gather | solution.py:46
  127.4 1.2 multiply_reduce_fusion.3
  128.7 1.2 convolution_multiply_fusion
  129.9 1.2 convolution_multiply_fusion.2
  131.2 1.2 convolution_multiply_fusion.4
  132.4 1.2 convolution_multiply_fusion.6
  133.6 0.0 copy-done.1
  133.6 1.4 divide_bitcast_fusion
  135.0 1.4 divide_bitcast_fusion.1
  136.4 1.4 divide_bitcast_fusion.2
  137.8 1.4 divide_bitcast_fusion.3
  139.2 2.3 %pad_maximum_fusion = f32[4,256,1024]{2,1,0:T(8,128)} fusion(f32[1,256,1024]{2,1,0:T(8,128)S(1)} %get-tuple-element.19, f32[1,256,1024]{2,1,0:T(8,128)S(1)} %get-tuple-element.16, f32[1,256,1024]{2,1,0:T(8,128)S(1)} %get-tuple-element.13, f32[1,256,1024]{2,1,0:T(8,128)S(1)} %get-tuple-element.10), kind=kLoop, calls=%fused_computation.1 | loop fusion | flops 3145728 | bytes 8388608 | tf_op jit(solution)/shard_map/stack | solution.py:57
  141.5 2.6 %maximum_maximum_fusion = bf16[4,2,256,1024]{3,2,1,0:T(8,128)(2,1)} fusion(bf16[1,1,256,1024]{3,2,1,0:T(8,128)(2,1)S(1)} %get-tuple-element.21, bf16[1,1,256,1024]{3,2,1,0:T(8,128)(2,1)S(1)} %get-tuple-element.20, bf16[1,1,256,1024]{3,2,1,0:T(8,128)(2,1)S(1)} %get-tuple-element.18, bf16[1,1,256,1024]{3,2,1,0:T(8,128)(2,1)S(1)} %get-tuple-element.17, ...), kind=kLoop, calls=%fused_computation | loop fusion | flops 14680064 | bytes 8388608 | tf_op jit(solution)/shard_map/stack | solution.py:57
  (6 shorter events, 0.1 us)
Async XLA Ops:
  7.2 2.1 %copy-start = (bf16[256,512]{1,0:T(8,128)(2,1)S(1)}, bf16[256,512]{1,0:T(8,128)(2,1)}, u32[]{:S(2)}) copy-start(bf16[256,512]{1,0:T(8,128)(2,1)} %param.2) | copy-start | bytes 786436
  7.2 120.3 %all-gather.2.cloned.1.call-start = ((), (), s32[]{:S(2)}) async-start(), calls=%async_computation | async-start | bytes 4325376 | tf_op jit(solution)/shard_map/all_gather | solution.py:46
  48.5 85.2 %copy-start.1 = (bf16[256,256]{0,1:T(8,128)(2,1)S(1)}, bf16[256,256]{0,1:T(8,128)(2,1)}, u32[]{:S(2)}) copy-start(bf16[256,256]{0,1:T(8,128)(2,1)} %all-reduce.1) | copy-start | bytes 393220
Sparse Core Ops, SparseCore 0:
  48.6 78.7 all-gather.1
where the time goes:
time: 151 us
  waiting for transfers between devices  77.2 us (51%)
  blocking collectives  38.9 us (26%)
  between operations  14.2 us (9%)
  matrix products  10.7 us (7%)
  other arithmetic  9.9 us (7%)
    all_gather x1, waiting for transfers between devices, body(): gathered = lax.all_gather(spectra, 'svc', axis=0, tiled=True)  77.2 us
    psum x1, blocking collectives, body(): spectra = lax.psum(partial_value, 'tm').astype(jnp.bfloat16)  38.9 us
    dot_general x4, matrix products, band_products(): lax.dot_general(row_spec, col_spec, dims, preferred_element_type=jnp.floa...  5.53 us
    another operation x2, other arithmetic, body(): return (jnp.stack(cross_list, axis=0), jnp.stack(coherence_list, axis=0))  4.9 us
    dot_general x4, matrix products, band_products(): lax.dot_general(swapped, col_spec, dims, preferred_element_type=jnp.float32)  4.89 us
  transfers between devices with their start and end apart: 1, of which 1 were waited for; matrix products, arithmetic and copies ran while one was open for 1% of the time, Pallas kernels for 0%

commit v1 on v0

--- a/solution.py
+++ b/solution.py
@@ -7,6 +7,13 @@
 BANDS = 4
 BINS = 32
 epsilon = 1e-06
+
+
+def swapped_in(x, axis, dim):
+    count = lax.axis_size(axis)
+    shards = jnp.stack([x for _ in range(count)])
+    shards = lax.all_to_all(shards, axis, split_axis=0, concat_axis=0)
+    return jnp.concatenate(shards, axis=dim)
 
 
 def make_table(minutes, band_starts):
@@ -43,7 +50,7 @@
     spectra = lax.psum(partial_value, "tm").astype(jnp.bfloat16)
     owners = lax.axis_size("svc") // lax.axis_size("tm")
     col_count = row_count * owners
-    gathered = lax.all_gather(spectra, "svc", axis=0, tiled=True)
+    gathered = swapped_in(spectra, "svc", 0)
     columns_panel = lax.dynamic_slice_in_dim(gathered, time_index * col_count, col_count, 0)
     cross_list = []
     coherence_list = []

time: 151 us -> 172 us (1.14)
  waiting for transfers between devices: 77.2 us -> 94.6 us
  starting transfers between devices: 0.04 us -> 16.8 us
  between operations: 14.2 us -> 0.86 us
  local copies, waits for them, and re-layouts: 0.01 us -> 10.8 us
  matrix products: 10.7 us -> 3.37 us
  other arithmetic: 9.9 us -> 7.17 us
    all_to_all x0 -> x1, waiting for transfers between devices: none -> 94.6 us  [swapped_in(): shards = lax.all_to_all(shards, axis, split_axis=0, concat_axis=0)]
    all_gather x1 -> x0, waiting for transfers between devices: 77.2 us -> none  [body(): gathered = lax.all_gather(spectra, 'svc', axis=0, tiled=True)]
    all_to_all x0 -> x1, starting transfers between devices: none -> 16.8 us  [swapped_in(): shards = lax.all_to_all(shards, axis, split_axis=0, concat_axis=0)]
    all_to_all x0 -> x1, local copies, waits for them, and re-layouts: none -> 6.4 us  [swapped_in(): shards = lax.all_to_all(shards, axis, split_axis=0, concat_axis=0)]
    dot_general x4, matrix products: 5.53 us -> 1.8 us  [band_products(): lax.dot_general(row_spec, col_spec, dims, preferred_element_type=jnp.floa...]
    dot_general x4, matrix products: 4.89 us -> 1.3 us  [band_products(): lax.dot_general(swapped, col_spec, dims, preferred_element_type=jnp.float32)]
    another operation x0 -> x1, local copies, waits for them, and re-layouts: none -> 2.49 us  [swapped_in(): shards = jnp.stack([x for _ in range(count)])]
    unnamed x4 -> x7, local copies, waits for them, and re-layouts: 0.01 us -> 1.96 us
  transfers between devices with their start and end apart: 1 -> 1, of which waited for: 1 -> 1; matrix products, arithmetic and copies ran while one was open for 1% -> 0% of each run, Pallas kernels for 0% -> 0%
where the time goes in v1:
time: 172 us
  waiting for transfers between devices  94.6 us (55%)
  blocking collectives  38.4 us (22%)
  starting transfers between devices  16.8 us (10%)
  local copies, waits for them, and re-layouts  10.8 us (6%)
  other arithmetic  7.17 us (4%)
  matrix products  3.37 us (2%)
    all_to_all x1, waiting for transfers between devices, swapped_in(): shards = lax.all_to_all(shards, axis, split_axis=0, concat_axis=0)  94.6 us
    psum x1, blocking collectives, body(): spectra = lax.psum(partial_value, 'tm').astype(jnp.bfloat16)  38.4 us
    all_to_all x1, starting transfers between devices, swapped_in(): shards = lax.all_to_all(shards, axis, split_axis=0, concat_axis=0)  16.8 us
    all_to_all x1, local copies, waits for them, and re-layouts, swapped_in(): shards = lax.all_to_all(shards, axis, split_axis=0, concat_axis=0)  6.4 us
    another operation x2, other arithmetic, body(): return (jnp.stack(cross_list, axis=0), jnp.stack(coherence_list, axis=0))  4.9 us
  transfers between devices with their start and end apart: 1, of which 1 were waited for; matrix products, arithmetic and copies ran while one was open for 0% of the time, Pallas kernels for 0%

profile of v1, /device:TPU:1, one launch (start us, length us, event | category | flops | bytes accessed | tf_op | source)
XLA Modules:
  0.0 172.0 jit_solution(16962961761272311974)
XLA Ops:
  0.6 0.0 copy-start
  0.7 0.8 iota_add_fusion
  1.4 1.2 multiply_convert_fusion.1
  2.7 0.3 convolution_bitcast_fusion
  3.0 38.4 %all-reduce.1 = bf16[256,256]{0,1:T(8,128)(2,1)S(1)} all-reduce(f32[256,256]{0,1:T(8,128)S(1)} %convolution_bitcast_fusion), channel_id=1, replica_groups=mesh['svc'=32,'tm'=8] {'tm'}, use_global_device_ids=true, to_apply=%region_0.1 | all-reduce | flops 65536 | bytes 393216 | tf_op jit(solution)/shard_map/psum | solution.py:50
  41.4 2.5 %stack.42 = bf16[32,256,256]{1,2,0:T(8,128)(2,1)} broadcast(bf16[256,256]{0,1:T(8,128)(2,1)S(1)} %all-reduce.1), dimensions={1,2} | broadcast | bytes 4325376 | tf_op jit(solution)/shard_map/stack | solution.py:14
  43.9 16.8 %all-to-all-start = ((bf16[32,256,256]{1,2,0:T(8,128)(2,1)}), bf16[32,256,256]{1,2,0:T(8,128)(2,1)}, u32[]{:S(2)}, u32[]{:S(2)}) async-start(bf16[32,256,256]{1,2,0:T(8,128)(2,1)} %stack.42), calls=%async_computation | async-start | bytes 8388608 | tf_op jit(solution)/shard_map/all_to_all | solution.py:15
  60.7 94.6 %all-to-all-done = bf16[32,256,256]{1,2,0:T(8,128)(2,1)} async-done(((bf16[32,256,256]{1,2,0:T(8,128)(2,1)}), bf16[32,256,256]{1,2,0:T(8,128)(2,1)}, u32[]{:S(2)}, u32[]{:S(2)}) %all-to-all-start) | async-done | bytes 4194336 | tf_op jit(solution)/shard_map/all_to_all | solution.py:15
  155.3 6.4 %copy.11 = bf16[32,256,256]{2,1,0:T(8,128)(2,1)} copy(bf16[32,256,256]{1,2,0:T(8,128)(2,1)} %all-to-all-done) | data formatting | bytes 8388608 | tf_op jit(solution)/shard_map/all_to_all | solution.py:15
  161.7 1.4 constant_dynamic-slice_fusion
  163.2 0.1 copy.14
  163.3 0.1 copy.16
  163.5 0.1 copy.15
  163.7 0.1 copy.17
  163.9 0.3 convolution_multiply_fusion.6
  164.3 0.3 convolution_multiply_fusion.2
  164.6 0.3 convolution_multiply_fusion.4
  164.9 0.3 convolution_multiply_fusion
  165.2 0.5 divide_bitcast_fusion.3
  165.7 0.5 divide_bitcast_fusion.1
  166.2 0.4 divide_bitcast_fusion.2
  166.6 0.5 divide_bitcast_fusion
  167.1 2.3 %pad_maximum_fusion = f32[4,256,1024]{2,1,0:T(8,128)} fusion(f32[1,256,1024]{2,1,0:T(8,128)S(1)} %get-tuple-element.19, f32[1,256,1024]{2,1,0:T(8,128)S(1)} %get-tuple-element.16, f32[1,256,1024]{2,1,0:T(8,128)S(1)} %get-tuple-element.13, f32[1,256,1024]{2,1,0:T(8,128)S(1)} %get-tuple-element.10), kind=kLoop, calls=%fused_computation.1 | loop fusion | flops 3145728 | bytes 8388608 | tf_op jit(solution)/shard_map/stack | solution.py:64
  169.4 2.6 %maximum_maximum_fusion = bf16[4,2,256,1024]{3,2,1,0:T(8,128)(2,1)} fusion(bf16[1,1,256,1024]{3,2,1,0:T(8,128)(2,1)S(1)} %get-tuple-element.21, bf16[1,1,256,1024]{3,2,1,0:T(8,128)(2,1)S(1)} %get-tuple-element.20, bf16[1,1,256,1024]{3,2,1,0:T(8,128)(2,1)S(1)} %get-tuple-element.18, bf16[1,1,256,1024]{3,2,1,0:T(8,128)(2,1)S(1)} %get-tuple-element.17, ...), kind=kLoop, calls=%fused_computation | loop fusion | flops 14680064 | bytes 8388608 | tf_op jit(solution)/shard_map/stack | solution.py:64
  (15 shorter events, 0.3 us)
Async XLA Ops:
  0.6 2.1 %copy-start = (bf16[256,512]{1,0:T(8,128)(2,1)S(1)}, bf16[256,512]{1,0:T(8,128)(2,1)}, u32[]{:S(2)}) copy-start(bf16[256,512]{1,0:T(8,128)(2,1)} %param.2) | copy-start | bytes 786436
  43.9 111.4 %all-to-all-start = ((bf16[32,256,256]{1,2,0:T(8,128)(2,1)}), bf16[32,256,256]{1,2,0:T(8,128)(2,1)}, u32[]{:S(2)}, u32[]{:S(2)}) async-start(bf16[32,256,256]{1,2,0:T(8,128)(2,1)} %stack.42), calls=%async_computation | async-start | bytes 8388608 | tf_op jit(solution)/shard_map/all_to_all | solution.py:15
